TPU v7x, 512 devices: a whole 4x4x16 slice. The times are simulated.
512 devices in a mesh: tm: 128 (over z, y, core), chan: 4 (over x).
Axes of the slice: x: 4, y: 4, z: 16, core: 2. Of those that a mesh axis runs over, the one named last changes fastest.
Arguments:
- series: bfloat16 [32768, 512], P('tm', 'chan'), may hold values from -6 to 6
- proj_weight: bfloat16 [512, 3, 512], P(None, None, 'chan'), may hold values from -0.25 to 0.25
- proj_bias: float32 [3, 512], P(None, 'chan'), may hold values from -6 to 6
- short_taps: float32 [3, 3, 512], P(None, None, 'chan'), may hold values from -6 to 6
- short_bias: float32 [3, 512], P(None, 'chan'), may hold values from -6 to 6
- spectrum: float32 [2, 128, 2, 256, 512], P(None, 'tm', None, None, 'chan'), may hold values from -6 to 6
- skip_gain: float32 [512], P('chan'), may hold values from -6 to 6
- out_weight: bfloat16 [512, 512], replicated, may hold values from -0.25 to 0.25
- out_bias: float32 [512], P('chan'), may hold values from -6 to 6
Outputs:
- mixed_out: bfloat16 [32768, 512], P('tm', 'chan')
All inputs are finite; a program needn't handle non-finite values.
Results may differ from a plain program's by a relative error of at most 0.009.
Values may be sent and summed in bfloat16 or wider, within the bound.
No kernel may reach another device: no remote copies, remote signals or barrier semaphores. Data moves between devices by JAX's collectives and lax.ppermute only.
A program may use at most 64 MiB of HBM per device.

v0:
```python
import math
import jax
import jax.numpy as jnp
import numpy as np
from jax import lax
from jax.sharding import PartitionSpec as P

HI = lax.Precision.HIGHEST


def from_behind(array, axis, by):
    length = lax.axis_size(axis)
    pairs = [(i, i + by) for i in range(length) if 0 <= i + by < length]
    return lax.ppermute(array, axis, pairs)


def reverse_bits_np(values, digits):
    result = np.zeros_like(values)
    for bit_level in range(digits):
        result = result | (values >> bit_level & 1) << digits - 1 - bit_level
    return result


def dft_tables(tm_count, steps_dev):
    rows = 2 * tm_count
    digits = tm_count.bit_length() - 1
    r = np.arange(rows)
    k1 = 2 * reverse_bits_np(r // 2, digits) + r % 2
    m = np.arange(tm_count)
    t = np.arange(steps_dev)
    b = np.arange(steps_dev)
    period = rows * steps_dev
    ang1 = 2 * np.pi * (k1[:, None] * m[None, :] % rows) / rows
    ang2 = 2 * np.pi * (t[:, None] * b[None, :] % steps_dev) / steps_dev
    angt = 2 * np.pi * (k1[:, None] * t[None, :] % period) / period
    f32 = lambda a: jnp.asarray(a.astype(np.float32))
    return dict(
        c1=f32(np.cos(ang1)),
        s1=f32(np.sin(ang1)),
        c2=f32(np.cos(ang2)),
        s2=f32(np.sin(ang2)),
        ct=f32(np.cos(angt)),
        st=f32(np.sin(angt)),
        period=period,
    )


def mm(a, b):
    return jnp.dot(a, b, precision=HI, preferred_element_type=jnp.float32)


def long_conv(x, h, tab):
    c1, s1, c2, s2, ct, st = (tab[k] for k in ("c1", "s1", "c2", "s2", "ct", "st"))
    ar = mm(c1, x)
    ai = -mm(s1, x)
    tr = ar * ct + ai * st
    ti = ai * ct - ar * st
    zr = mm(tr, c2) + mm(ti, s2)
    zi = mm(ti, c2) - mm(tr, s2)
    yr = h[0] * zr - h[1] * zi
    yi = h[0] * zi + h[1] * zr
    br = mm(yr, c2) - mm(yi, s2)
    bi = mm(yi, c2) + mm(yr, s2)
    ur = br * ct - bi * st
    ui = bi * ct + br * st
    y = lax.dot_general(
        c1, ur, (((0,), (0,)), ((), ())), precision=HI, preferred_element_type=jnp.float32
    )
    y = y - lax.dot_general(
        s1, ui, (((0,), (0,)), ((), ())), precision=HI, preferred_element_type=jnp.float32
    )
    return y * (1.0 / tab["period"])


def shards(
    series,
    proj_weight,
    proj_bias,
    short_taps,
    short_bias,
    spectrum,
    skip_gain,
    out_weight,
    out_bias,
):
    steps_dev = series.shape[0]
    model_width = proj_weight.shape[0]
    channels = proj_weight.shape[2]
    tm_count = lax.axis_size("tm")
    tab = dft_tables(tm_count, steps_dev)
    flat_weight = proj_weight.reshape(model_width, 3 * channels)
    projected = jnp.dot(
        lax.all_gather(series, "chan", axis=1, tiled=True),
        flat_weight,
        preferred_element_type=jnp.float32,
    )
    projected = (projected.reshape(steps_dev, 3, channels) + proj_bias).astype(jnp.bfloat16)
    taps_count = short_taps.shape[0]
    earlier = from_behind(projected[steps_dev - taps_count + 1 :], "tm", 1)
    extended = jnp.concatenate([earlier, projected], 0).astype(jnp.float32)
    streams = short_bias + short_taps[0] * extended[taps_count - 1 :]
    for offset in range(1, taps_count):
        streams = (
            streams
            + short_taps[offset]
            * extended[taps_count - 1 - offset : taps_count - 1 - offset + steps_dev]
        )
    streams = streams.astype(jnp.bfloat16)
    gate_out = streams[:, 0]
    mixed_in = (streams[:, 1].astype(jnp.float32) * streams[:, 2].astype(jnp.float32)).astype(
        jnp.bfloat16
    )
    pair = jnp.stack([mixed_in, gate_out])[:, None]
    pair = lax.all_to_all(pair, "tm", 3, 1, tiled=True)
    signal_bf = pair[0, :, :, 0]
    gate_own = pair[1, :, :, 0].astype(jnp.float32)
    h = lax.all_to_all(spectrum, "tm", 4, 1, tiled=True)
    h = h.reshape(2, 2 * tm_count, steps_dev)
    signal = signal_bf.astype(jnp.float32)
    convolved = long_conv(signal, h, tab)
    skip = lax.dynamic_index_in_dim(skip_gain, lax.axis_index("tm"), 0, keepdims=False)
    gated = ((convolved + skip * signal) * gate_own).astype(jnp.bfloat16)
    gated = lax.all_to_all(gated[:, :, None], "tm", 0, 2, tiled=True)
    gated = lax.all_gather(gated[0], "chan", axis=1, tiled=True)
    column_start = lax.axis_index("chan") * channels
    weight_cols = lax.dynamic_slice_in_dim(out_weight, column_start, channels, 1)
    mixed_out = jnp.dot(gated, weight_cols, preferred_element_type=jnp.float32) + out_bias
    return mixed_out.astype(jnp.bfloat16)


def solution(mesh):
    return jax.shard_map(
        shards,
        mesh=mesh,
        in_specs=(
            P("tm", "chan"),
            P(None, None, "chan"),
            P(None, "chan"),
            P(None, None, "chan"),
            P(None, "chan"),
            P(None, "tm", None, None, "chan"),
            P("chan"),
            P(),
            P("chan"),
        ),
        out_specs=P("tm", "chan"),
        check_vma=False,
    )
```

profile of v0, /device:TPU:2, one launch (start us, length us, event | category | flops | bytes accessed | tf_op | source)
XLA Modules:
  0.0 140.7 jit_solution(8496077110473266639)
XLA Ops:
  0.0 0.0 copy-start
  0.0 1.2 copy.32
  1.2 0.0 copy-done.13
  1.2 0.0 copy-start.15
  1.3 15.2 %all_gather.6 = bf16[256,512]{1,0:T(8,128)(2,1)S(1)} all-gather(bf16[256,128]{1,0:T(8,128)(2,1)S(1)} %copy-done.13), channel_id=1, replica_groups=mesh['tm'=128,'chan'=4] {'chan'}, dimensions={1}, use_global_device_ids=true | all-gather | bytes 327680 | tf_op jit(solution)/shard_map/all_gather | solution.py:93
  16.4 0.0 copy-done.15
  16.4 0.3 fusion
  16.8 1.3 collective-permute-start
  18.1 0.0 copy-done.14
  18.1 0.8 collective-permute-done
  18.9 0.0 copy-start.16
  18.9 0.7 copy-done.16
  19.6 0.1 fusion.9
  19.8 0.0 copy-start.10
  19.8 0.8 copy.33
  20.6 20.5 %all-to-all-start.1 = ((bf16[2,1,256,128]{2,0,1,3:T(2,128)(2,1)}), bf16[2,1,256,128]{2,0,1,3:T(2,128)(2,1)S(1)}, u32[]{:S(2)}, u32[]{:S(2)}) async-start(bf16[2,1,256,128]{2,0,1,3:T(2,128)(2,1)} %copy.33), calls=%async_computation.1 | async-start | bytes 262144 | tf_op jit(solution)/shard_map/all_to_all | solution.py:114
  41.1 0.0 copy-done.10
  41.1 1.0 copy.31
  42.1 14.4 %all-to-all-done.1 = bf16[2,1,256,128]{2,0,1,3:T(2,128)(2,1)S(1)} async-done(((bf16[2,1,256,128]{2,0,1,3:T(2,128)(2,1)}), bf16[2,1,256,128]{2,0,1,3:T(2,128)(2,1)S(1)}, u32[]{:S(2)}, u32[]{:S(2)}) %all-to-all-start.1) | async-done | bytes 131104 | tf_op jit(solution)/shard_map/all_to_all | solution.py:114
  56.5 7.8 %all-to-all-start = ((f32[2,1,2,256,128]{3,2,1,0,4:T(2,128)}), f32[2,1,2,256,128]{3,2,1,0,4:T(2,128)S(1)}, u32[]{:S(2)}, u32[]{:S(2)}) async-start(f32[2,1,2,256,128]{3,2,1,0,4:T(2,128)} %copy.31), calls=%async_computation | async-start | bytes 1048576 | tf_op jit(solution)/shard_map/all_to_all | solution.py:117
  64.3 0.0 copy-start.18
  64.4 0.6 copy-done.18
  65.0 0.6 dynamic_slice.7
  65.6 0.1 copy.34
  65.7 0.8 copy-done.11
  66.5 0.3 convolution_negate_fusion
  66.8 0.0 copy-done.8
  66.8 0.0 copy-start.2
  66.8 0.3 fusion.26
  67.1 0.4 copy-done.3
  67.5 0.1 copy-done.6
  67.5 0.2 copy-done.2
  67.8 0.4 fusion.23
  68.2 0.6 copy-done.1
  68.7 0.1 copy-done.5
  68.8 1.1 fusion.24
  69.9 0.0 copy-done.4
  69.9 0.4 convolution_add_fusion.2
  70.3 24.9 %all-to-all-done = f32[2,1,2,256,128]{3,2,1,0,4:T(2,128)S(1)} async-done(((f32[2,1,2,256,128]{3,2,1,0,4:T(2,128)}), f32[2,1,2,256,128]{3,2,1,0,4:T(2,128)S(1)}, u32[]{:S(2)}, u32[]{:S(2)}) %all-to-all-start) | async-done | bytes 524320 | tf_op jit(solution)/shard_map/all_to_all | solution.py:117
  95.2 0.2 fusion.28
  95.4 0.2 squeeze.23
  95.6 0.0 copy-start.7
  95.6 0.2 squeeze.21
  95.8 0.8 copy-done.7
  96.6 1.4 multiply_subtract_fusion
  97.9 0.4 fusion.30
  98.3 0.4 fusion.29
  98.7 0.4 convolution_add_fusion.1
  99.1 0.0 copy-start.9
  99.1 0.4 convolution_subtract_fusion
  99.5 0.5 copy-done.9
  100.0 0.6 fusion.18
  100.6 0.3 copy-done.12
  100.9 1.2 fusion.7
  102.1 0.1 copy.36
  102.3 0.5 broadcast.5
  102.8 1.0 reduce
  103.8 0.7 reshape.55
  104.5 9.0 %all-to-all-start.2 = ((bf16[128,2,128]{2,1,0:T(2,128)(2,1)}), bf16[128,2,128]{2,1,0:T(2,128)(2,1)S(1)}, u32[]{:S(2)}, u32[]{:S(2)}) async-start(bf16[128,2,128]{2,1,0:T(2,128)(2,1)} %reshape.55), calls=%async_computation.2 | async-start | bytes 131072 | tf_op jit(solution)/shard_map/all_to_all | solution.py:123
  113.5 14.5 %all-to-all-done.2 = bf16[128,2,128]{2,1,0:T(2,128)(2,1)S(1)} async-done(((bf16[128,2,128]{2,1,0:T(2,128)(2,1)}), bf16[128,2,128]{2,1,0:T(2,128)(2,1)S(1)}, u32[]{:S(2)}, u32[]{:S(2)}) %all-to-all-start.2) | async-done | bytes 65568 | tf_op jit(solution)/shard_map/all_to_all | solution.py:123
  128.0 0.0 copy-start.17
  128.0 11.8 %all-gather = bf16[1,256,512,1]{1,2,3,0:T(8,128)(2,1)S(1)} all-gather(bf16[1,256,128,1]{1,2,3,0:T(8,128)(2,1)S(1)} %bitcast.98), channel_id=2, replica_groups=mesh['tm'=128,'chan'=4] {'chan'}, dimensions={2}, use_global_device_ids=true | all-gather | bytes 327680 | tf_op jit(solution)/shard_map/all_gather | solution.py:124
  139.8 0.0 copy-done
  139.8 0.9 fusion.6
  (19 shorter events, 0.2 us)
Async XLA Ops:
  0.0 139.8 %copy-start = (bf16[512,512]{1,0:T(8,128)(2,1)S(1)}, bf16[512,512]{1,0:T(8,128)(2,1)}, u32[]{:S(2)}) copy-start(bf16[512,512]{1,0:T(8,128)(2,1)} %param.22) | copy-start | bytes 1572868
  0.0 1.2 copy-start.13
  1.2 15.2 %copy-start.15 = (f32[3,128]{1,0:T(4,128)S(1)}, f32[3,128]{1,0:T(4,128)}, u32[]{:S(2)}) copy-start(f32[3,128]{1,0:T(4,128)} %param.17) | copy-start | bytes 4612
  16.4 1.6 %copy-start.14 = (f32[3,3,128]{2,1,0:T(4,128)S(1)}, f32[3,3,128]{2,1,0:T(4,128)}, u32[]{:S(2)}) copy-start(f32[3,3,128]{2,1,0:T(4,128)} %param.18) | copy-start | bytes 13828
  16.8 2.1 %collective-permute-start = (bf16[2,3,128]{2,0,1:T(2,128)(2,1)S(1)}, bf16[2,3,128]{2,0,1:T(2,128)(2,1)S(1)}, u32[]{:S(2)}, u32[]{:S(2)}) collective-permute-start(bf16[2,3,128]{2,0,1:T(2,128)(2,1)S(1)} %slice.63), channel_id=1, source_target_pairs={{0,4},{4,8},{8,12},{12,16},{16,20},{20,24},{24,28},{28,32},{32,36}... | collective-permute-start | bytes 4616 | tf_op jit(solution)/shard_map/ppermute | solution.py:14
  18.9 0.7 copy-start.16
  19.8 21.4 %copy-start.10 = (f32[2,1,2,256,128]{4,3,2,1,0:T(8,128)S(1)}, f32[2,1,2,256,128]{4,3,2,1,0:T(8,128)}, u32[]{:S(2)}) copy-start(f32[2,1,2,256,128]{4,3,2,1,0:T(8,128)} %param.20) | copy-start | bytes 1572868
  20.6 35.9 %all-to-all-start.1 = ((bf16[2,1,256,128]{2,0,1,3:T(2,128)(2,1)}), bf16[2,1,256,128]{2,0,1,3:T(2,128)(2,1)S(1)}, u32[]{:S(2)}, u32[]{:S(2)}) async-start(bf16[2,1,256,128]{2,0,1,3:T(2,128)(2,1)} %copy.33), calls=%async_computation.1 | async-start | bytes 262144 | tf_op jit(solution)/shard_map/all_to_all | solution.py:114
  56.5 38.7 %all-to-all-start = ((f32[2,1,2,256,128]{3,2,1,0,4:T(2,128)}), f32[2,1,2,256,128]{3,2,1,0,4:T(2,128)S(1)}, u32[]{:S(2)}, u32[]{:S(2)}) async-start(f32[2,1,2,256,128]{3,2,1,0,4:T(2,128)} %copy.31), calls=%async_computation | async-start | bytes 1048576 | tf_op jit(solution)/shard_map/all_to_all | solution.py:117
  64.3 0.7 copy-start.18
  65.6 0.9 copy-start.11
  65.6 1.2 copy-start.8
  66.5 1.0 copy-start.3
  66.5 1.0 copy-start.6
  66.8 1.0 copy-start.2
  67.8 0.9 copy-start.1
  67.8 1.0 copy-start.5
  68.8 1.1 copy-start.4
  95.6 1.0 copy-start.7
  99.1 0.9 copy-start.9
  100.0 0.9 copy-start.12
  104.5 23.5 %all-to-all-start.2 = ((bf16[128,2,128]{2,1,0:T(2,128)(2,1)}), bf16[128,2,128]{2,1,0:T(2,128)(2,1)S(1)}, u32[]{:S(2)}, u32[]{:S(2)}) async-start(bf16[128,2,128]{2,1,0:T(2,128)(2,1)} %reshape.55), calls=%async_computation.2 | async-start | bytes 131072 | tf_op jit(solution)/shard_map/all_to_all | solution.py:123
  128.0 11.8 %copy-start.17 = (f32[128]{0:T(128)S(1)}, f32[128]{0:T(128)}, u32[]{:S(2)}) copy-start(f32[128]{0:T(128)} %param.23) | copy-start | bytes 1540
where the time goes:
time: 141 us
  waiting for transfers between devices  54.5 us (39%)
  starting transfers between devices  38.6 us (27%)
  blocking collectives  26.9 us (19%)
  local copies, waits for them, and re-layouts  10.7 us (8%)
  matrix products  8.38 us (6%)
    all_to_all x1, waiting for transfers between devices, shards(): h = lax.all_to_all(spectrum, 'tm', 4, 1, tiled=True)  24.9 us
    all_to_all x1, starting transfers between devices, shards(): pair = lax.all_to_all(pair, 'tm', 3, 1, tiled=True)  20.5 us
    all_gather x1, blocking collectives, shards(): lax.all_gather(series, 'chan', axis=1, tiled=True)  15.2 us
    all_to_all x1, waiting for transfers between devices, shards(): gated = lax.all_to_all(gated[:, :, None], 'tm', 0, 2, tiled=True)  14.5 us
    all_to_all x1, waiting for transfers between devices, shards(): pair = lax.all_to_all(pair, 'tm', 3, 1, tiled=True)  14.4 us
    all_gather x1, blocking collectives, shards(): gated = lax.all_gather(gated[0], 'chan', axis=1, tiled=True)  11.8 us
    all_to_all x1, starting transfers between devices, shards(): gated = lax.all_to_all(gated[:, :, None], 'tm', 0, 2, tiled=True)  9.02 us
    unnamed x44, local copies, waits for them, and re-layouts  8.47 us
  transfers between devices with their start and end apart: 4, of which 4 were waited for; matrix products, arithmetic and copies ran while one was open for 3% of the time, Pallas kernels for 0%

commit v1 on v0

--- a/solution.py
+++ b/solution.py
@@ -121,7 +121,13 @@
     skip = lax.dynamic_index_in_dim(skip_gain, lax.axis_index("tm"), 0, keepdims=False)
     gated = ((convolved + skip * signal) * gate_own).astype(jnp.bfloat16)
     gated = lax.all_to_all(gated[:, :, None], "tm", 0, 2, tiled=True)
-    gated = lax.all_gather(gated[0], "chan", axis=1, tiled=True)
+    perform_the_spans = lambda sample: jnp.concatenate(
+        lax.all_to_all(
+            jnp.stack([sample for _ in range(lax.axis_size("chan"))], axis=0), "chan", 0, 0
+        ),
+        axis=1,
+    )
+    gated = perform_the_spans(gated[0])
     column_start = lax.axis_index("chan") * channels
     weight_cols = lax.dynamic_slice_in_dim(out_weight, column_start, channels, 1)
     mixed_out = jnp.dot(gated, weight_cols, preferred_element_type=jnp.float32) + out_bias

time: 141 us -> 139 us (0.986)
  the two profiles are of different devices: /device:TPU:2 before, /device:TPU:1 now
where the time goes in v1:
time: 139 us
  waiting for transfers between devices  48.6 us (35%)
  starting transfers between devices  35.3 us (25%)
  blocking collectives  34.2 us (25%)
  local copies, waits for them, and re-layouts  10.8 us (8%)
  matrix products  8.38 us (6%)
    all_to_all x1, waiting for transfers between devices, shards(): h = lax.all_to_all(spectrum, 'tm', 4, 1, tiled=True)  24.7 us
    all_to_all x1, blocking collectives, shards(): gated = lax.all_to_all(gated[:, :, None], 'tm', 0, 2, tiled=True)  23.9 us
    all_to_all x1, starting transfers between devices, shards(): pair = lax.all_to_all(pair, 'tm', 3, 1, tiled=True)  18.2 us
    all_to_all x1, waiting for transfers between devices, shards(): pair = lax.all_to_all(pair, 'tm', 3, 1, tiled=True)  15 us
    all_gather x1, blocking collectives, shards(): lax.all_gather(series, 'chan', axis=1, tiled=True)  10.3 us
    unnamed x44, local copies, waits for them, and re-layouts  7.84 us
    all_to_all x1, starting transfers between devices, shards(): h = lax.all_to_all(spectrum, 'tm', 4, 1, tiled=True)  7.23 us
    ppermute x1, starting transfers between devices, from_behind(): return lax.ppermute(array, axis, pairs)  6.27 us
  transfers between devices with their start and end apart: 4, of which 4 were waited for; matrix products, arithmetic and copies ran while one was open for 3% of the time, Pallas kernels for 0%

profile of v1, /device:TPU:1, one launch (start us, length us, event | category | flops | bytes accessed | tf_op | source)
XLA Modules:
  0.0 138.8 jit_solution(14367658271972884744)
XLA Ops:
  0.0 0.0 copy-start
  0.0 1.2 copy.33
  1.2 0.0 copy-done.13
  1.2 0.0 copy-start.15
  1.3 10.3 %all_gather.3 = bf16[256,512]{1,0:T(8,128)(2,1)S(1)} all-gather(bf16[256,128]{1,0:T(8,128)(2,1)S(1)} %copy-done.13), channel_id=1, replica_groups=mesh['tm'=128,'chan'=4] {'chan'}, dimensions={1}, use_global_device_ids=true | all-gather | bytes 327680 | tf_op jit(solution)/shard_map/all_gather | solution.py:93
  11.6 0.0 copy-done.15
  11.6 0.3 fusion
  11.9 6.3 %collective-permute-start = (bf16[2,3,128]{2,0,1:T(2,128)(2,1)S(1)}, bf16[2,3,128]{2,0,1:T(2,128)(2,1)S(1)}, u32[]{:S(2)}, u32[]{:S(2)}) collective-permute-start(bf16[2,3,128]{2,0,1:T(2,128)(2,1)S(1)} %slice.63), channel_id=1, source_target_pairs={{0,4},{4,8},{8,12},{12,16},{16,20},{20,24},{24,28},{28,32},{32,36}... | collective-permute-start | bytes 4616 | tf_op jit(solution)/shard_map/ppermute | solution.py:14
  18.2 0.0 copy-done.14
  18.2 3.3 %collective-permute-done = bf16[2,3,128]{2,0,1:T(2,128)(2,1)S(1)} collective-permute-done((bf16[2,3,128]{2,0,1:T(2,128)(2,1)S(1)}, bf16[2,3,128]{2,0,1:T(2,128)(2,1)S(1)}, u32[]{:S(2)}, u32[]{:S(2)}) %collective-permute-start) | collective-permute-done | bytes 1568 | tf_op jit(solution)/shard_map/ppermute | solution.py:14
  21.5 0.0 copy-start.16
  21.6 0.7 copy-done.16
  22.2 0.1 fusion.9
  22.4 0.0 copy-start.10
  22.5 0.8 copy.34
  23.3 18.2 %all-to-all-start.1 = ((bf16[2,1,256,128]{2,0,1,3:T(2,128)(2,1)}), bf16[2,1,256,128]{2,0,1,3:T(2,128)(2,1)S(1)}, u32[]{:S(2)}, u32[]{:S(2)}) async-start(bf16[2,1,256,128]{2,0,1,3:T(2,128)(2,1)} %copy.34), calls=%async_computation.1 | async-start | bytes 262144 | tf_op jit(solution)/shard_map/all_to_all | solution.py:114
  41.5 0.0 copy-done.10
  41.5 1.0 copy.32
  42.5 15.0 %all-to-all-done.1 = bf16[2,1,256,128]{2,0,1,3:T(2,128)(2,1)S(1)} async-done(((bf16[2,1,256,128]{2,0,1,3:T(2,128)(2,1)}), bf16[2,1,256,128]{2,0,1,3:T(2,128)(2,1)S(1)}, u32[]{:S(2)}, u32[]{:S(2)}) %all-to-all-start.1) | async-done | bytes 131104 | tf_op jit(solution)/shard_map/all_to_all | solution.py:114
  57.5 7.2 %all-to-all-start = ((f32[2,1,2,256,128]{3,2,1,0,4:T(2,128)}), f32[2,1,2,256,128]{3,2,1,0,4:T(2,128)S(1)}, u32[]{:S(2)}, u32[]{:S(2)}) async-start(f32[2,1,2,256,128]{3,2,1,0,4:T(2,128)} %copy.32), calls=%async_computation | async-start | bytes 1048576 | tf_op jit(solution)/shard_map/all_to_all | solution.py:117
  64.7 0.0 copy-start.18
  64.7 0.6 copy-done.18
  65.4 0.6 dynamic_slice.7
  66.0 0.1 copy.35
  66.1 0.8 copy-done.11
  66.9 0.3 convolution_negate_fusion
  67.1 0.0 copy-done.8
  67.2 0.0 copy-start.2
  67.2 0.3 fusion.25
  67.4 0.4 copy-done.3
  67.8 0.1 copy-done.6
  67.9 0.2 copy-done.2
  68.2 0.4 fusion.22
  68.5 0.5 copy-done.1
  69.1 0.1 copy-done.5
  69.2 1.1 fusion.23
  70.3 0.0 copy-done.4
  70.3 0.4 convolution_add_fusion.2
  70.7 24.7 %all-to-all-done = f32[2,1,2,256,128]{3,2,1,0,4:T(2,128)S(1)} async-done(((f32[2,1,2,256,128]{3,2,1,0,4:T(2,128)}), f32[2,1,2,256,128]{3,2,1,0,4:T(2,128)S(1)}, u32[]{:S(2)}, u32[]{:S(2)}) %all-to-all-start) | async-done | bytes 524320 | tf_op jit(solution)/shard_map/all_to_all | solution.py:117
  95.4 0.2 fusion.27
  95.6 0.2 squeeze.20
  95.8 0.0 copy-start.7
  95.8 0.2 squeeze.18
  96.0 0.8 copy-done.7
  96.7 1.4 multiply_subtract_fusion
  98.1 0.4 fusion.29
  98.5 0.4 fusion.28
  98.9 0.4 convolution_add_fusion.1
  99.2 0.0 copy-start.9
  99.3 0.4 convolution_subtract_fusion
  99.6 0.5 copy-done.9
  100.2 0.6 fusion.17
  100.8 0.3 copy-done.12
  101.1 1.2 fusion.7
  102.3 0.1 copy.37
  102.5 0.5 broadcast.6
  103.0 1.0 reduce
  104.0 23.9 %all_to_all.53 = bf16[128,2,128]{2,1,0:T(2,128)(2,1)S(1)} all-to-all(bf16[128,2,128]{2,1,0:T(2,128)(2,1)S(1)} %reshape.63), channel_id=1, replica_groups=mesh['tm'=128,'chan'=4] {'tm'}, dimensions={0} | all-to-all | bytes 131072 | tf_op jit(solution)/shard_map/all_to_all | solution.py:123
  128.0 0.7 stack.8
  128.7 3.5 %all-to-all-start.3 = ((bf16[4,256,128]{1,2,0:T(8,128)(2,1)}), bf16[4,256,128]{1,2,0:T(8,128)(2,1)S(1)}, u32[]{:S(2)}, u32[]{:S(2)}) async-start(bf16[4,256,128]{1,2,0:T(8,128)(2,1)} %stack.8), calls=%async_computation.3 | async-start | bytes 524288 | tf_op jit(solution)/shard_map/all_to_all | solution.py:125
  132.2 5.6 %all-to-all-done.3 = bf16[4,256,128]{1,2,0:T(8,128)(2,1)S(1)} async-done(((bf16[4,256,128]{1,2,0:T(8,128)(2,1)}), bf16[4,256,128]{1,2,0:T(8,128)(2,1)S(1)}, u32[]{:S(2)}, u32[]{:S(2)}) %all-to-all-start.3) | async-done | bytes 262176 | tf_op jit(solution)/shard_map/all_to_all | solution.py:125
  137.9 0.0 copy-done
  137.9 0.0 copy-done.17
  137.9 0.9 fusion.6
  (20 shorter events, 0.2 us)
Async XLA Ops:
  0.0 137.9 %copy-start = (bf16[512,512]{1,0:T(8,128)(2,1)S(1)}, bf16[512,512]{1,0:T(8,128)(2,1)}, u32[]{:S(2)}) copy-start(bf16[512,512]{1,0:T(8,128)(2,1)} %param.22) | copy-start | bytes 1572868
  0.0 1.2 copy-start.13
  1.2 10.3 %copy-start.15 = (f32[3,128]{1,0:T(4,128)S(1)}, f32[3,128]{1,0:T(4,128)}, u32[]{:S(2)}) copy-start(f32[3,128]{1,0:T(4,128)} %param.17) | copy-start | bytes 4612
  11.6 6.6 %copy-start.14 = (f32[3,3,128]{2,1,0:T(4,128)S(1)}, f32[3,3,128]{2,1,0:T(4,128)}, u32[]{:S(2)}) copy-start(f32[3,3,128]{2,1,0:T(4,128)} %param.18) | copy-start | bytes 13828
  11.9 9.6 %collective-permute-start = (bf16[2,3,128]{2,0,1:T(2,128)(2,1)S(1)}, bf16[2,3,128]{2,0,1:T(2,128)(2,1)S(1)}, u32[]{:S(2)}, u32[]{:S(2)}) collective-permute-start(bf16[2,3,128]{2,0,1:T(2,128)(2,1)S(1)} %slice.63), channel_id=1, source_target_pairs={{0,4},{4,8},{8,12},{12,16},{16,20},{20,24},{24,28},{28,32},{32,36}... | collective-permute-start | bytes 4616 | tf_op jit(solution)/shard_map/ppermute | solution.py:14
  21.5 0.7 copy-start.16
  22.4 19.1 %copy-start.10 = (f32[2,1,2,256,128]{4,3,2,1,0:T(8,128)S(1)}, f32[2,1,2,256,128]{4,3,2,1,0:T(8,128)}, u32[]{:S(2)}) copy-start(f32[2,1,2,256,128]{4,3,2,1,0:T(8,128)} %param.20) | copy-start | bytes 1572868
  23.3 34.2 %all-to-all-start.1 = ((bf16[2,1,256,128]{2,0,1,3:T(2,128)(2,1)}), bf16[2,1,256,128]{2,0,1,3:T(2,128)(2,1)S(1)}, u32[]{:S(2)}, u32[]{:S(2)}) async-start(bf16[2,1,256,128]{2,0,1,3:T(2,128)(2,1)} %copy.34), calls=%async_computation.1 | async-start | bytes 262144 | tf_op jit(solution)/shard_map/all_to_all | solution.py:114
  57.5 37.9 %all-to-all-start = ((f32[2,1,2,256,128]{3,2,1,0,4:T(2,128)}), f32[2,1,2,256,128]{3,2,1,0,4:T(2,128)S(1)}, u32[]{:S(2)}, u32[]{:S(2)}) async-start(f32[2,1,2,256,128]{3,2,1,0,4:T(2,128)} %copy.32), calls=%async_computation | async-start | bytes 1048576 | tf_op jit(solution)/shard_map/all_to_all | solution.py:117
  64.7 0.7 copy-start.18
  66.0 0.9 copy-start.11
  66.0 1.2 copy-start.8
  66.9 1.0 copy-start.3
  66.9 1.0 copy-start.6
  67.2 1.0 copy-start.2
  68.1 0.9 copy-start.1
  68.1 1.0 copy-start.5
  69.2 1.1 copy-start.4
  95.8 1.0 copy-start.7
  99.2 0.9 copy-start.9
  100.2 0.9 copy-start.12
  128.7 9.2 %all-to-all-start.3 = ((bf16[4,256,128]{1,2,0:T(8,128)(2,1)}), bf16[4,256,128]{1,2,0:T(8,128)(2,1)S(1)}, u32[]{:S(2)}, u32[]{:S(2)}) async-start(bf16[4,256,128]{1,2,0:T(8,128)(2,1)} %stack.8), calls=%async_computation.3 | async-start | bytes 524288 | tf_op jit(solution)/shard_map/all_to_all | solution.py:125
  132.2 5.6 %copy-start.17 = (f32[128]{0:T(128)S(1)}, f32[128]{0:T(128)}, u32[]{:S(2)}) copy-start(f32[128]{0:T(128)} %param.23) | copy-start | bytes 1540
